TPU v7x, 32 devices: a whole 2x2x4 slice. The times are simulated.
32 devices in a mesh: groups: 2 (over y), lat: 4 (over x, core), lon: 4 (over z).
Axes of the slice: x: 2, y: 2, z: 4, core: 2. Of those that a mesh axis runs over, the one named last changes fastest.
Arguments:
- fields: bfloat16 [512, 4, 512], P('groups', 'lat', 'lon'), parts along dimension 0, may hold values from -6 to 6
- upstream: bfloat16 [512, 4, 512], P('groups', 'lat', 'lon'), parts along dimension 0, may hold values from -6 to 6
- weights: bfloat16 [9, 256, 256], replicated, may hold values from -0.125 to 0.125
- filter_taps: bfloat16 [4, 9, 3, 2, 64], P('lat'), may hold values from -0.3125 to 0.3125
- cycle_counts: int32 [4], P('lat'), may hold values from 1 to 2, as said below
- cycle_blocks: int32 [4, 2], P('lat'), may hold values from -2 to 1, as said below
Outputs:
- outputs: bfloat16 [512, 4, 512], P('groups', 'lat', 'lon'), parts along dimension 0
- input_grad: bfloat16 [512, 4, 512], P('groups', 'lat', 'lon'), parts along dimension 0
- weight_grad: float32 [18, 256, 256], P('groups', 'lon'), parts along dimension 0
There are 2 independent parts, one for each index of `groups`. A program takes and returns all parts, laid end to end along the dimension named above; an argument that names none is the same for every part. Nothing has to cross between parts.
Inputs may be any that keep to these rules, and one draw needn't show every extreme that they name: Cycle i uses its first cycle_counts[i] slots; the first quarter of the cycles (at least one) uses all 2, the last cycle one. `cycle_blocks`: the 2 block numbers of a cycle are distinct; the first cycle holds the lowest and the highest.
All inputs are finite; a program needn't handle non-finite values.
Results may differ from a plain program's by a relative error of at most 0.0049.
Values may be sent and summed in bfloat16 or wider, within the bound.
No kernel may reach another device: no remote copies, remote signals or barrier semaphores. Data moves between devices by JAX's collectives and lax.ppermute only.
A program may use at most 64 MiB of HBM per device.

v0:
```python
import jax
import jax.numpy as jnp
from jax import lax
from jax.sharding import PartitionSpec as P

HALO = 128


def padded_2(cells, sides, width, closed):
    for axis, dim in sides:
        count = lax.axis_size(axis)
        ends = count if closed else count - 1
        head = lax.slice_in_dim(cells, 0, width, axis=dim)
        tail = lax.slice_in_dim(cells, cells.shape[dim] - width, cells.shape[dim], axis=dim)
        cells = jnp.concatenate(
            [
                lax.ppermute(tail, axis, [(i, (i + 1) % count) for i in range(ends)]),
                cells,
                lax.ppermute(head, axis, [((i + 1) % count, i) for i in range(ends)]),
            ],
            axis=dim,
        )
    return cells


def build_taps(filter_taps, cycle_counts, cycle_blocks):
    slot_total = cycle_blocks.shape[1]
    width_block = filter_taps.shape[4]
    offsets = jnp.arange(width_block, dtype=jnp.int32)
    places = HALO + width_block * cycle_blocks[:, :, None] + offsets[None, None, :]
    live_slots = jnp.arange(slot_total, dtype=jnp.int32)[None, :] < cycle_counts[:, None]
    positions = jnp.arange(2 * HALO, dtype=jnp.int32)
    onehot = jnp.where(
        (places[:, :, :, None] == positions) & live_slots[:, :, None, None], 1.0, 0.0
    ).astype(jnp.float32)
    return jnp.einsum("ikrst,istu->ikru", filter_taps.astype(jnp.float32), onehot)


def banded_matrix(tap_row, out_width, tap_reach):
    kernels = tap_row.shape[0]
    stencil_rows = tap_row.shape[1]
    window_len = out_width + tap_reach
    padded = jnp.concatenate(
        [tap_row, jnp.zeros((kernels, stencil_rows, window_len + 1 - tap_reach), tap_row.dtype)],
        axis=2,
    )
    repeated = jnp.tile(padded, (1, 1, out_width))[:, :, : out_width * window_len]
    repeated = repeated.reshape(kernels, stencil_rows, out_width, window_len)
    return jnp.transpose(repeated, (1, 3, 0, 2))


def body(fields, upstream, weights, filter_taps, cycle_counts, cycle_blocks):
    channels, lat_rows, lon_cols = fields.shape
    kernels = weights.shape[0]
    window_len = lon_cols + 2 * HALO
    tap_table = build_taps(filter_taps, cycle_counts, cycle_blocks).astype(jnp.bfloat16)
    banded = padded_2(fields, (("lat", 1),), 1, False)
    widened = padded_2(banded, (("lon", 2),), HALO, True)
    matrices = [
        banded_matrix(tap_table[0], lon_cols, 2 * HALO).reshape(3 * window_len, kernels * lon_cols)
    ]
    cycle_row = 0
    responses = [
        jnp.dot(
            widened.reshape(channels, 3 * window_len),
            matrices[cycle_row],
            preferred_element_type=jnp.float32,
        )
    ]
    response = (
        jnp.stack(responses, axis=1)
        .reshape(channels, lat_rows, kernels, lon_cols)
        .astype(jnp.bfloat16)
    )
    outputs = jnp.einsum(
        "koc,cikj->oij", weights, response, preferred_element_type=jnp.float32
    ).astype(jnp.bfloat16)
    response_grad = jnp.einsum(
        "koc,oij->cikj", weights, upstream, preferred_element_type=jnp.float32
    ).astype(jnp.bfloat16)
    grad_terms = jnp.einsum("oij,cikj->koc", upstream, response, preferred_element_type=jnp.float32)
    grad_share = lax.psum_scatter(grad_terms, "lon", scatter_dimension=1, tiled=True)
    weight_grad = lax.psum(grad_share, "lat")
    accumulated = jnp.zeros((channels, lat_rows + 2, window_len), jnp.float32)
    cycle_row = 0
    grad_piece = response_grad[:, cycle_row].reshape(channels, kernels * lon_cols)
    contrib = jnp.einsum(
        "cn,mn->cm", grad_piece, matrices[cycle_row], preferred_element_type=jnp.float32
    )
    accumulated = accumulated.at[:, cycle_row : cycle_row + 3].add(
        contrib.reshape(channels, 3, window_len)
    )
    rim_columns = jnp.concatenate(
        [accumulated[:, :, :HALO], accumulated[:, :, HALO + lon_cols :]], axis=2
    )
    arrived = padded_2(rim_columns, (("lon", 2),), HALO, True)
    interior = accumulated[:, :, HALO : HALO + lon_cols]
    interior = interior.at[:, :, :HALO].add(arrived[:, :, :HALO])
    interior = interior.at[:, :, lon_cols - HALO :].add(arrived[:, :, 3 * HALO :])
    edge_rows = jnp.stack([interior[:, 0], interior[:, lat_rows + 1]], axis=1)
    arrived = padded_2(edge_rows, (("lat", 1),), 1, False)
    result = interior[:, 1 : lat_rows + 1]
    result = result.at[:, 0].add(arrived[:, 0])
    result = result.at[:, lat_rows - 1].add(arrived[:, 3])
    return (outputs, result.astype(jnp.bfloat16), weight_grad)


def solution(mesh):
    return jax.shard_map(
        body,
        mesh=mesh,
        in_specs=(
            P("groups", "lat", "lon"),
            P("groups", "lat", "lon"),
            P(),
            P("lat", None, None, None, None),
            P("lat"),
            P("lat", None),
        ),
        out_specs=(P("groups", "lat", "lon"), P("groups", "lat", "lon"), P("groups", "lon", None)),
        check_vma=False,
    )
```

profile of v0, /device:TPU:0, one launch (start us, length us, event | category | flops | bytes accessed | tf_op | source)
XLA Modules:
  0.0 197.8 jit_solution(18379826614206599920)
XLA Ops:
  7.2 0.0 copy-start
  7.2 0.0 reduce-scatter.2.cloned.1.call-start
  7.2 1.0 copy.32
  8.3 1.3 collective-permute-start.1
  9.6 3.0 %collective-permute-start = (bf16[256,1,128]{0,2,1:T(8,128)(2,1)S(1)}, bf16[256,1,128]{0,2,1:T(8,128)(2,1)S(1)}, u32[]{:S(2)}, u32[]{:S(2)}) collective-permute-start(bf16[256,1,128]{0,2,1:T(8,128)(2,1)S(1)} %copy.32), channel_id=1, source_target_pairs={{0,4},{4,8},{8,12},{1,5},{5,9},{9,13},{2,6},{6,10},{10,14},{3,7},{... | collective-permute-start | bytes 196616 | tf_op jit(solution)/shard_map/ppermute | solution.py:17
  13.2 0.7 add_bitcast_fusion
  13.9 0.1 iota_add_fusion
  14.0 0.0 collective-permute-done
  14.0 5.1 %collective-permute-start.3 = (bf16[256,3,128]{0,2,1:T(8,128)(2,1)S(1)}, bf16[256,3,128]{0,2,1:T(8,128)(2,1)S(1)}, u32[]{:S(2)}, u32[]{:S(2)}) collective-permute-start(bf16[256,3,128]{0,2,1:T(8,128)(2,1)S(1)} %pad_maximum_fusion.1), channel_id=1, source_target_pairs={{1,0},{2,1},{3,2},{0,3},{5,4},{6,5},{7,6},{4,7},{9,8},{10,9},{11,1... | collective-permute-start | bytes 589832 | tf_op jit(solution)/shard_map/ppermute | solution.py:19
  19.1 0.9 fusion.3
  20.1 2.1 %tile.4 = bf16[9,3,128,385]{3,2,1,0:T(8,128)(2,1)} broadcast(bf16[9,3,385]{2,1,0:T(4,128)(2,1)S(1)} %concatenate.21.clone), dimensions={0,1,3} | broadcast | bytes 2681910 | tf_op jit(solution)/shard_map/tile | solution.py:47
  22.2 11.0 %tile.10 = bf16[9,3,49280]{2,1,0:T(4,128)(2,1)} reshape(bf16[9,3,128,385]{3,2,1,0:T(8,128)(2,1)} %tile.4) | data formatting | bytes 5322240 | tf_op jit(solution)/shard_map/tile | solution.py:47
  33.2 5.1 %slice.123 = bf16[9,3,49152]{2,1,0:T(4,128)(2,1)} slice(bf16[9,3,49280]{2,1,0:T(4,128)(2,1)} %tile.10), slice={[0:9], [0:3], [0:49152]} | slice | bytes 5308416 | tf_op jit(solution)/shard_map/slice | solution.py:47
  38.3 8.2 %reshape.267 = bf16[9,3,128,384]{3,2,1,0:T(8,128)(2,1)} reshape(bf16[9,3,49152]{2,1,0:T(4,128)(2,1)} %slice.123) | data formatting | bytes 5308416 | tf_op jit(solution)/shard_map/reshape | solution.py:48
  46.6 4.0 %copy.37 = bf16[3,384,9,128]{1,0,3,2:T(4,128)(2,1)S(1)} copy(bf16[3,384,9,128]{1,3,0,2:T(8,128)(2,1)} %bitcast.68) | data formatting | bytes 5308416 | tf_op jit(solution)/shard_map/transpose | solution.py:49
  50.6 0.5 copy.57
  51.1 0.0 collective-permute-done.3
  51.1 0.0 collective-permute-done.2
  51.2 0.0 copy-start.3
  51.2 1.1 convolution_convert_fusion.1
  52.3 0.0 copy-start.1
  52.3 0.8 copy-done.1
  53.1 0.5 convolution_bitcast_fusion
  53.6 3.4 %copy.44 = f32[9,256,256]{2,0,1:T(8,128)} copy(f32[9,256,256]{1,2,0:T(8,128)S(1)} %convolution_bitcast_fusion) | data formatting | bytes 4718592 | tf_op jit(solution)/shard_map/oij,cikj->koc/transpose | solution.py:81
  57.0 0.0 reduce-scatter.2.cloned.1.call-update
  57.0 0.0 copy-start.4
  57.0 0.0 all-reduce.3.cloned.1.call-start
  57.1 2.0 %copy.41 = bf16[3,384,9,128]{1,3,2,0:T(8,128)(2,1)S(1)} copy(bf16[3,384,9,128]{1,3,0,2:T(8,128)(2,1)} %bitcast.69) | data formatting | bytes 5308416 | tf_op jit(solution)/shard_map/transpose | solution.py:49
  59.1 0.3 convolution_convert_fusion
  59.5 1.0 fusion.22
  60.5 0.1 fusion.20
  60.6 0.1 collective-permute-start.4
  60.6 3.9 %collective-permute-start.5 = (f32[256,3,128]{2,0,1:T(8,128)S(1)}, f32[256,3,128]{2,0,1:T(8,128)S(1)}, u32[]{:S(2)}, u32[]{:S(2)}) collective-permute-start(f32[256,3,128]{2,0,1:T(8,128)S(1)} %get-tuple-element.97), channel_id=1, source_target_pairs={{1,0},{2,1},{3,2},{0,3},{5,4},{6,5},{7,6},{4,7},{9,8},{10,9},{11,1... | collective-permute-start | bytes 1179656 | tf_op jit(solution)/shard_map/ppermute | solution.py:19
  64.5 14.1 %collective-permute-done.4 = f32[256,3,128]{2,0,1:T(8,128)S(1)} collective-permute-done((f32[256,3,128]{2,0,1:T(8,128)S(1)}, f32[256,3,128]{2,0,1:T(8,128)S(1)}, u32[]{:S(2)}, u32[]{:S(2)}) %collective-permute-start.4) | collective-permute-done | bytes 393248 | tf_op jit(solution)/shard_map/ppermute | solution.py:17
  78.6 14.9 %collective-permute-done.5 = f32[256,3,128]{2,0,1:T(8,128)S(1)} collective-permute-done((f32[256,3,128]{2,0,1:T(8,128)S(1)}, f32[256,3,128]{2,0,1:T(8,128)S(1)}, u32[]{:S(2)}, u32[]{:S(2)}) %collective-permute-start.5) | collective-permute-done | bytes 393248 | tf_op jit(solution)/shard_map/ppermute | solution.py:19
  93.5 0.1 fusion.4
  93.6 0.0 copy-start.2
  93.6 1.5 collective-permute-start.6
  95.1 1.3 collective-permute-start.7
  96.4 53.4 %reduce-scatter.2.cloned.1.call-done = f32[9,64,256]{2,0,1:T(8,128)} async-done(((f32[9,256,256]{2,0,1:T(8,128)}), f32[9,64,256]{2,0,1:T(8,128)}) %reduce-scatter.2.cloned.1.call-update) | async-done | bytes 589840 | tf_op jit(solution)/shard_map/reduce_scatter | solution.py:82
  149.8 0.0 all-reduce.3.cloned.1.call-update
  149.8 0.5 fusion.1
  150.3 0.7 copy.45
  151.1 0.0 collective-permute-done.6
  151.1 0.0 collective-permute-done.7
  151.1 0.7 fusion.6
  151.7 36.9 %all-reduce.3.cloned.1.call-done = f32[9,64,256]{2,0,1:T(8,128)} async-done(((f32[9,64,256]{2,0,1:T(8,128)}), f32[9,64,256]{2,0,1:T(8,128)}) %all-reduce.3.cloned.1.call-update) | async-done | bytes 589840 | tf_op jit(solution)/shard_map/psum | solution.py:83
  188.6 2.4 %copy.46 = f32[9,64,256]{2,1,0:T(8,128)} copy(f32[9,64,256]{2,0,1:T(8,128)} %all-reduce.3.cloned.1.call-done) | data formatting | bytes 1179648
  (12 shorter events, 0.1 us)
Async XLA Ops:
  7.2 51.9 %copy-start = (bf16[9,256,256]{2,1,0:T(8,128)(2,1)S(1)}, bf16[9,256,256]{2,1,0:T(8,128)(2,1)}, u32[]{:S(2)}) copy-start(bf16[9,256,256]{2,1,0:T(8,128)(2,1)} %param.24) | copy-start | bytes 3538948
  7.2 142.6 %reduce-scatter.2.cloned.1.call-start = ((), (), s32[]{:S(2)}) async-start(), calls=%async_computation.1 | async-start | bytes 5242880 | tf_op jit(solution)/shard_map/reduce_scatter | solution.py:82
  8.3 5.7 %collective-permute-start.1 = (bf16[256,1,128]{0,2,1:T(8,128)(2,1)S(1)}, bf16[256,1,128]{0,2,1:T(8,128)(2,1)S(1)}, u32[]{:S(2)}, u32[]{:S(2)}) collective-permute-start(bf16[256,1,128]{0,2,1:T(8,128)(2,1)S(1)} %copy.32), channel_id=1, source_target_pairs={{4,0},{8,4},{12,8},{5,1},{9,5},{13,9},{6,2},{10,6},{14,10},{7,3},{... | collective-permute-start | bytes 196616 | tf_op jit(solution)/shard_map/ppermute | solution.py:19
  9.6 4.4 %collective-permute-start = (bf16[256,1,128]{0,2,1:T(8,128)(2,1)S(1)}, bf16[256,1,128]{0,2,1:T(8,128)(2,1)S(1)}, u32[]{:S(2)}, u32[]{:S(2)}) collective-permute-start(bf16[256,1,128]{0,2,1:T(8,128)(2,1)S(1)} %copy.32), channel_id=1, source_target_pairs={{0,4},{4,8},{8,12},{1,5},{5,9},{9,13},{2,6},{6,10},{10,14},{3,7},{... | collective-permute-start | bytes 196616 | tf_op jit(solution)/shard_map/ppermute | solution.py:17
  14.0 37.1 %collective-permute-start.3 = (bf16[256,3,128]{0,2,1:T(8,128)(2,1)S(1)}, bf16[256,3,128]{0,2,1:T(8,128)(2,1)S(1)}, u32[]{:S(2)}, u32[]{:S(2)}) collective-permute-start(bf16[256,3,128]{0,2,1:T(8,128)(2,1)S(1)} %pad_maximum_fusion.1), channel_id=1, source_target_pairs={{1,0},{2,1},{3,2},{0,3},{5,4},{6,5},{7,6},{4,7},{9,8},{10,9},{11,1... | collective-permute-start | bytes 589832 | tf_op jit(solution)/shard_map/ppermute | solution.py:19
  19.1 32.0 %collective-permute-start.2 = (bf16[256,3,128]{0,2,1:T(8,128)(2,1)S(1)}, bf16[256,3,128]{0,2,1:T(8,128)(2,1)S(1)}, u32[]{:S(2)}, u32[]{:S(2)}) collective-permute-start(bf16[256,3,128]{0,2,1:T(8,128)(2,1)S(1)} %pad_maximum_fusion.1), channel_id=1, source_target_pairs={{0,1},{1,2},{2,3},{3,0},{4,5},{5,6},{6,7},{7,4},{8,9},{9,10},{10,1... | collective-permute-start | bytes 589832 | tf_op jit(solution)/shard_map/ppermute | solution.py:17
  51.2 1.9 copy-start.3
  52.3 0.8 copy-start.1
  57.0 2.1 %copy-start.4 = (bf16[256,1,128]{2,0,1:T(8,128)(2,1)S(1)}, bf16[256,1,128]{2,0,1:T(8,128)(2,1)}, u32[]{:S(2)}) copy-start(bf16[256,1,128]{2,0,1:T(8,128)(2,1)} %param.23) | copy-start | bytes 196612
  57.0 131.6 %all-reduce.3.cloned.1.call-start = ((), (), s32[]{:S(2)}) async-start(), calls=%async_computation.2 | async-start | bytes 2097152 | tf_op jit(solution)/shard_map/psum | solution.py:83
  60.6 18.0 %collective-permute-start.4 = (f32[256,3,128]{2,0,1:T(8,128)S(1)}, f32[256,3,128]{2,0,1:T(8,128)S(1)}, u32[]{:S(2)}, u32[]{:S(2)}) collective-permute-start(f32[256,3,128]{2,0,1:T(8,128)S(1)} %get-tuple-element.96), channel_id=1, source_target_pairs={{0,1},{1,2},{2,3},{3,0},{4,5},{5,6},{6,7},{7,4},{8,9},{9,10},{10,1... | collective-permute-start | bytes 1179656 | tf_op jit(solution)/shard_map/ppermute | solution.py:17
  60.6 32.9 %collective-permute-start.5 = (f32[256,3,128]{2,0,1:T(8,128)S(1)}, f32[256,3,128]{2,0,1:T(8,128)S(1)}, u32[]{:S(2)}, u32[]{:S(2)}) collective-permute-start(f32[256,3,128]{2,0,1:T(8,128)S(1)} %get-tuple-element.97), channel_id=1, source_target_pairs={{1,0},{2,1},{3,2},{0,3},{5,4},{6,5},{7,6},{4,7},{9,8},{10,9},{11,1... | collective-permute-start | bytes 1179656 | tf_op jit(solution)/shard_map/ppermute | solution.py:19
  93.6 56.2 %copy-start.2 = (bf16[256,9,128]{2,0,1:T(8,128)(2,1)S(1)}, bf16[256,9,128]{2,0,1:T(8,128)(2,1)}, u32[]{:S(2)}) copy-start(bf16[256,9,128]{2,0,1:T(8,128)(2,1)} %copy-done.1) | copy-start | bytes 1769476
  93.6 57.5 %collective-permute-start.6 = (f32[256,1,128]{2,0,1:T(8,128)S(1)}, f32[256,1,128]{2,0,1:T(8,128)S(1)}, u32[]{:S(2)}, u32[]{:S(2)}) collective-permute-start(f32[256,1,128]{2,0,1:T(8,128)S(1)} %get-tuple-element.98), channel_id=1, source_target_pairs={{0,4},{4,8},{8,12},{1,5},{5,9},{9,13},{2,6},{6,10},{10,14},{3,7},{... | collective-permute-start | bytes 393224 | tf_op jit(solution)/shard_map/ppermute | solution.py:17
  95.1 56.0 %collective-permute-start.7 = (f32[256,1,128]{2,0,1:T(8,128)S(1)}, f32[256,1,128]{2,0,1:T(8,128)S(1)}, u32[]{:S(2)}, u32[]{:S(2)}) collective-permute-start(f32[256,1,128]{2,0,1:T(8,128)S(1)} %get-tuple-element.99), channel_id=1, source_target_pairs={{4,0},{8,4},{12,8},{5,1},{9,5},{13,9},{6,2},{10,6},{14,10},{7,3},{... | collective-permute-start | bytes 393224 | tf_op jit(solution)/shard_map/ppermute | solution.py:19
Sparse Core Ops, SparseCore 0:
  57.1 92.6 reduce-scatter.1
  152.2 36.3 all-reduce.2
where the time goes:
time: 199 us; the launch traced here: 198 us
  waiting for transfers between devices  119 us (60%)
  local copies, waits for them, and re-layouts  41.5 us (21%)
  starting transfers between devices  16.2 us (8%)
  between operations  14.9 us (7%)
  matrix products  4.39 us (2%)
    reduce_scatter x1, waiting for transfers between devices, body(): lax.psum_scatter(grad_terms, 'lon', scatter_dimension=1, tiled=True)  53.4 us
    psum x1, waiting for transfers between devices, body(): weight_grad = lax.psum(grad_share, 'lat')  36.9 us
    ppermute x4, waiting for transfers between devices, padded_2(): lax.ppermute(head, axis, [((i + 1) % count, i) for i in range(ends)])  14.9 us
    ppermute x4, waiting for transfers between devices, padded_2(): lax.ppermute(tail, axis, [(i, (i + 1) % count) for i in range(ends)])  14.1 us
    another operation x2, local copies, waits for them, and re-layouts, banded_matrix(): jnp.tile(padded, (1, 1, out_width))[:, :, :out_width * window_len]  13.1 us
    ppermute x4, starting transfers between devices, padded_2(): lax.ppermute(head, axis, [((i + 1) % count, i) for i in range(ends)])  11.6 us
    reshape x1, local copies, waits for them, and re-layouts, banded_matrix(): repeated = repeated.reshape(kernels, stencil_rows, out_width, window_len)  8.24 us
    transpose x2, local copies, waits for them, and re-layouts, banded_matrix(): return jnp.transpose(repeated, (1, 3, 0, 2))  6.08 us
  transfers between devices with their start and end apart: 10, of which 4 were waited for; matrix products, arithmetic and copies ran while one was open for 19% of the time, Pallas kernels for 0%

commit v1 on v0

--- a/solution.py
+++ b/solution.py
@@ -80,7 +80,7 @@
     ).astype(jnp.bfloat16)
     grad_terms = jnp.einsum("oij,cikj->koc", upstream, response, preferred_element_type=jnp.float32)
     grad_share = lax.psum_scatter(grad_terms, "lon", scatter_dimension=1, tiled=True)
-    weight_grad = lax.psum(grad_share, "lat")
+    weight_grad = jax.lax.all_gather(grad_share, "lat").sum(axis=0)
     accumulated = jnp.zeros((channels, lat_rows + 2, window_len), jnp.float32)
     cycle_row = 0
     grad_piece = response_grad[:, cycle_row].reshape(channels, kernels * lon_cols)

time: 199 us -> 185 us (0.930)
  the two profiles are of different devices: /device:TPU:0 before, /device:TPU:1 now
where the time goes in v1:
time: 185 us; the launch traced here: 184 us
  waiting for transfers between devices  99.6 us (54%)
  local copies, waits for them, and re-layouts  41.6 us (22%)
  starting transfers between devices  18.9 us (10%)
  between operations  14.9 us (8%)
  matrix products  4.4 us (2%)
  other arithmetic  4.24 us (2%)
    reduce_scatter x1, waiting for transfers between devices, body(): lax.psum_scatter(grad_terms, 'lon', scatter_dimension=1, tiled=True)  79.1 us
    another operation x2, local copies, waits for them, and re-layouts, banded_matrix(): jnp.tile(padded, (1, 1, out_width))[:, :, :out_width * window_len]  13.1 us
    ppermute x4, waiting for transfers between devices, padded_2(): lax.ppermute(head, axis, [((i + 1) % count, i) for i in range(ends)])  11.9 us
    ppermute x4, starting transfers between devices, padded_2(): lax.ppermute(tail, axis, [(i, (i + 1) % count) for i in range(ends)])  9.54 us
    ppermute x4, starting transfers between devices, padded_2(): lax.ppermute(head, axis, [((i + 1) % count, i) for i in range(ends)])  9.29 us
    ppermute x4, waiting for transfers between devices, padded_2(): lax.ppermute(tail, axis, [(i, (i + 1) % count) for i in range(ends)])  8.61 us
    reshape x1, local copies, waits for them, and re-layouts, banded_matrix(): repeated = repeated.reshape(kernels, stencil_rows, out_width, window_len)  8.24 us
    transpose x2, local copies, waits for them, and re-layouts, banded_matrix(): return jnp.transpose(repeated, (1, 3, 0, 2))  6.11 us
  transfers between devices with their start and end apart: 10, of which 4 were waited for; matrix products, arithmetic and copies ran while one was open for 21% of the time, Pallas kernels for 0%

profile of v1, /device:TPU:1, one launch (start us, length us, event | category | flops | bytes accessed | tf_op | source)
XLA Modules:
  0.0 183.7 jit_solution(18091772679872770563)
XLA Ops:
  7.2 0.0 copy-start
  7.2 0.0 reduce-scatter.2.cloned.1.call-start
  7.2 1.0 copy.30
  8.3 2.0 %collective-permute-start.1 = (bf16[256,1,128]{0,2,1:T(8,128)(2,1)S(1)}, bf16[256,1,128]{0,2,1:T(8,128)(2,1)S(1)}, u32[]{:S(2)}, u32[]{:S(2)}) collective-permute-start(bf16[256,1,128]{0,2,1:T(8,128)(2,1)S(1)} %copy.30), channel_id=1, source_target_pairs={{4,0},{8,4},{12,8},{5,1},{9,5},{13,9},{6,2},{10,6},{14,10},{7,3},{... | collective-permute-start | bytes 196616 | tf_op jit(solution)/shard_map/ppermute | solution.py:19
  10.2 4.5 %collective-permute-start = (bf16[256,1,128]{0,2,1:T(8,128)(2,1)S(1)}, bf16[256,1,128]{0,2,1:T(8,128)(2,1)S(1)}, u32[]{:S(2)}, u32[]{:S(2)}) collective-permute-start(bf16[256,1,128]{0,2,1:T(8,128)(2,1)S(1)} %copy.30), channel_id=1, source_target_pairs={{0,4},{4,8},{8,12},{1,5},{5,9},{9,13},{2,6},{6,10},{10,14},{3,7},{... | collective-permute-start | bytes 196616 | tf_op jit(solution)/shard_map/ppermute | solution.py:17
  15.3 0.7 add_bitcast_fusion
  16.0 0.1 iota_add_fusion
  16.1 0.0 collective-permute-done.1
  16.1 0.0 collective-permute-done
  16.1 3.4 %collective-permute-start.3 = (bf16[256,3,128]{0,2,1:T(8,128)(2,1)S(1)}, bf16[256,3,128]{0,2,1:T(8,128)(2,1)S(1)}, u32[]{:S(2)}, u32[]{:S(2)}) collective-permute-start(bf16[256,3,128]{0,2,1:T(8,128)(2,1)S(1)} %pad_maximum_fusion.1), channel_id=1, source_target_pairs={{1,0},{2,1},{3,2},{0,3},{5,4},{6,5},{7,6},{4,7},{9,8},{10,9},{11,1... | collective-permute-start | bytes 589832 | tf_op jit(solution)/shard_map/ppermute | solution.py:19
  19.5 0.0 collective-permute-start.2
  19.5 0.9 fusion.3
  20.5 2.1 %tile.4 = bf16[9,3,128,385]{3,2,1,0:T(8,128)(2,1)} broadcast(bf16[9,3,385]{2,1,0:T(4,128)(2,1)S(1)} %concatenate.21.clone), dimensions={0,1,3} | broadcast | bytes 2681910 | tf_op jit(solution)/shard_map/tile | solution.py:47
  22.5 11.0 %tile.10 = bf16[9,3,49280]{2,1,0:T(4,128)(2,1)} reshape(bf16[9,3,128,385]{3,2,1,0:T(8,128)(2,1)} %tile.4) | data formatting | bytes 5322240 | tf_op jit(solution)/shard_map/tile | solution.py:47
  33.6 5.1 %slice.123 = bf16[9,3,49152]{2,1,0:T(4,128)(2,1)} slice(bf16[9,3,49280]{2,1,0:T(4,128)(2,1)} %tile.10), slice={[0:9], [0:3], [0:49152]} | slice | bytes 5308416 | tf_op jit(solution)/shard_map/slice | solution.py:47
  38.7 8.2 %reshape.267 = bf16[9,3,128,384]{3,2,1,0:T(8,128)(2,1)} reshape(bf16[9,3,49152]{2,1,0:T(4,128)(2,1)} %slice.123) | data formatting | bytes 5308416 | tf_op jit(solution)/shard_map/reshape | solution.py:48
  46.9 4.0 %copy.35 = bf16[3,384,9,128]{1,0,3,2:T(4,128)(2,1)S(1)} copy(bf16[3,384,9,128]{1,3,0,2:T(8,128)(2,1)} %bitcast.69) | data formatting | bytes 5308416 | tf_op jit(solution)/shard_map/transpose | solution.py:49
  51.0 0.5 copy.58
  51.5 0.0 collective-permute-done.3
  51.5 0.0 copy-start.3
  51.5 1.1 convolution_convert_fusion.1
  52.6 0.0 copy-start.1
  52.7 0.8 copy-done.1
  53.5 0.5 convolution_bitcast_fusion
  53.9 3.4 %copy.42 = f32[9,256,256]{2,0,1:T(8,128)} copy(f32[9,256,256]{1,2,0:T(8,128)S(1)} %convolution_bitcast_fusion) | data formatting | bytes 4718592 | tf_op jit(solution)/shard_map/oij,cikj->koc/transpose | solution.py:81
  57.4 0.0 reduce-scatter.2.cloned.1.call-update
  57.4 0.0 all-gather.3.cloned.1.call-start
  57.4 79.1 %reduce-scatter.2.cloned.1.call-done = f32[9,64,256]{2,0,1:T(8,128)} async-done(((f32[9,256,256]{2,0,1:T(8,128)}), f32[9,64,256]{2,0,1:T(8,128)}) %reduce-scatter.2.cloned.1.call-update) | async-done | bytes 589840 | tf_op jit(solution)/shard_map/reduce_scatter | solution.py:82
  136.6 2.4 %copy.43 = f32[9,64,256]{2,1,0:T(8,128)} copy(f32[9,64,256]{2,0,1:T(8,128)} %reduce-scatter.2.cloned.1.call-done) | data formatting | bytes 1179648 | tf_op jit(solution)/shard_map/reduce_scatter | solution.py:82
  139.0 0.0 all-gather.3.cloned.1.call-update
  139.0 0.0 copy-start.4
  139.0 2.1 %copy.39 = bf16[3,384,9,128]{1,3,2,0:T(8,128)(2,1)S(1)} copy(bf16[3,384,9,128]{1,3,0,2:T(8,128)(2,1)} %bitcast.70) | data formatting | bytes 5308416 | tf_op jit(solution)/shard_map/transpose | solution.py:49
  141.1 0.3 convolution_convert_fusion
  141.5 1.0 fusion.22
  142.5 0.1 fusion.20
  142.6 0.0 copy-start.2
  142.6 1.3 collective-permute-start.4
  143.9 2.0 %collective-permute-start.5 = (f32[256,3,128]{2,0,1:T(8,128)S(1)}, f32[256,3,128]{2,0,1:T(8,128)S(1)}, u32[]{:S(2)}, u32[]{:S(2)}) collective-permute-start(f32[256,3,128]{2,0,1:T(8,128)S(1)} %get-tuple-element.97), channel_id=1, source_target_pairs={{1,0},{2,1},{3,2},{0,3},{5,4},{6,5},{7,6},{4,7},{9,8},{10,9},{11,1... | collective-permute-start | bytes 1179656 | tf_op jit(solution)/shard_map/ppermute | solution.py:19
  145.9 8.6 %collective-permute-done.4 = f32[256,3,128]{2,0,1:T(8,128)S(1)} collective-permute-done((f32[256,3,128]{2,0,1:T(8,128)S(1)}, f32[256,3,128]{2,0,1:T(8,128)S(1)}, u32[]{:S(2)}, u32[]{:S(2)}) %collective-permute-start.4) | collective-permute-done | bytes 393248 | tf_op jit(solution)/shard_map/ppermute | solution.py:17
  154.5 8.8 %collective-permute-done.5 = f32[256,3,128]{2,0,1:T(8,128)S(1)} collective-permute-done((f32[256,3,128]{2,0,1:T(8,128)S(1)}, f32[256,3,128]{2,0,1:T(8,128)S(1)}, u32[]{:S(2)}, u32[]{:S(2)}) %collective-permute-start.5) | collective-permute-done | bytes 393248 | tf_op jit(solution)/shard_map/ppermute | solution.py:19
  163.3 0.1 fusion.4
  163.4 3.8 %collective-permute-start.6 = (f32[256,1,128]{2,0,1:T(8,128)S(1)}, f32[256,1,128]{2,0,1:T(8,128)S(1)}, u32[]{:S(2)}, u32[]{:S(2)}) collective-permute-start(f32[256,1,128]{2,0,1:T(8,128)S(1)} %get-tuple-element.98), channel_id=1, source_target_pairs={{0,4},{4,8},{8,12},{1,5},{5,9},{9,13},{2,6},{6,10},{10,14},{3,7},{... | collective-permute-start | bytes 393224 | tf_op jit(solution)/shard_map/ppermute | solution.py:17
  167.2 1.9 %collective-permute-start.7 = (f32[256,1,128]{2,0,1:T(8,128)S(1)}, f32[256,1,128]{2,0,1:T(8,128)S(1)}, u32[]{:S(2)}, u32[]{:S(2)}) collective-permute-start(f32[256,1,128]{2,0,1:T(8,128)S(1)} %get-tuple-element.99), channel_id=1, source_target_pairs={{4,0},{8,4},{12,8},{5,1},{9,5},{13,9},{6,2},{10,6},{14,10},{7,3},{... | collective-permute-start | bytes 393224 | tf_op jit(solution)/shard_map/ppermute | solution.py:19
  169.1 0.6 fusion.1
  169.7 0.7 copy.45
  170.4 3.1 %collective-permute-done.7 = f32[256,1,128]{2,0,1:T(8,128)S(1)} collective-permute-done((f32[256,1,128]{2,0,1:T(8,128)S(1)}, f32[256,1,128]{2,0,1:T(8,128)S(1)}, u32[]{:S(2)}, u32[]{:S(2)}) %collective-permute-start.7) | collective-permute-done | bytes 131104 | tf_op jit(solution)/shard_map/ppermute | solution.py:19
  173.5 0.7 fusion.6
  174.1 2.7 %reduce_sum.9 = f32[9,64,256]{2,1,0:T(8,128)} reduce(f32[4,9,64,256]{3,2,1,0:T(8,128)} %bitcast.74, f32[]{:T(128)} %constant.148.clone.1), dimensions={0}, to_apply=%region_1.2 | reduce | flops 442368 | bytes 2949124 | tf_op jit(solution)/shard_map/reduce_sum | solution.py:83
  (13 shorter events, 0.1 us)
Async XLA Ops:
  7.2 133.9 %copy-start = (bf16[9,256,256]{2,1,0:T(8,128)(2,1)S(1)}, bf16[9,256,256]{2,1,0:T(8,128)(2,1)}, u32[]{:S(2)}) copy-start(bf16[9,256,256]{2,1,0:T(8,128)(2,1)} %param.24) | copy-start | bytes 3538948
  7.2 129.4 %reduce-scatter.2.cloned.1.call-start = ((), (), s32[]{:S(2)}) async-start(), calls=%async_computation.1 | async-start | bytes 5242880 | tf_op jit(solution)/shard_map/reduce_scatter | solution.py:82
  8.3 7.8 %collective-permute-start.1 = (bf16[256,1,128]{0,2,1:T(8,128)(2,1)S(1)}, bf16[256,1,128]{0,2,1:T(8,128)(2,1)S(1)}, u32[]{:S(2)}, u32[]{:S(2)}) collective-permute-start(bf16[256,1,128]{0,2,1:T(8,128)(2,1)S(1)} %copy.30), channel_id=1, source_target_pairs={{4,0},{8,4},{12,8},{5,1},{9,5},{13,9},{6,2},{10,6},{14,10},{7,3},{... | collective-permute-start | bytes 196616 | tf_op jit(solution)/shard_map/ppermute | solution.py:19
  10.2 5.9 %collective-permute-start = (bf16[256,1,128]{0,2,1:T(8,128)(2,1)S(1)}, bf16[256,1,128]{0,2,1:T(8,128)(2,1)S(1)}, u32[]{:S(2)}, u32[]{:S(2)}) collective-permute-start(bf16[256,1,128]{0,2,1:T(8,128)(2,1)S(1)} %copy.30), channel_id=1, source_target_pairs={{0,4},{4,8},{8,12},{1,5},{5,9},{9,13},{2,6},{6,10},{10,14},{3,7},{... | collective-permute-start | bytes 196616 | tf_op jit(solution)/shard_map/ppermute | solution.py:17
  16.1 35.3 %collective-permute-start.3 = (bf16[256,3,128]{0,2,1:T(8,128)(2,1)S(1)}, bf16[256,3,128]{0,2,1:T(8,128)(2,1)S(1)}, u32[]{:S(2)}, u32[]{:S(2)}) collective-permute-start(bf16[256,3,128]{0,2,1:T(8,128)(2,1)S(1)} %pad_maximum_fusion.1), channel_id=1, source_target_pairs={{1,0},{2,1},{3,2},{0,3},{5,4},{6,5},{7,6},{4,7},{9,8},{10,9},{11,1... | collective-permute-start | bytes 589832 | tf_op jit(solution)/shard_map/ppermute | solution.py:19
  19.5 32.0 %collective-permute-start.2 = (bf16[256,3,128]{0,2,1:T(8,128)(2,1)S(1)}, bf16[256,3,128]{0,2,1:T(8,128)(2,1)S(1)}, u32[]{:S(2)}, u32[]{:S(2)}) collective-permute-start(bf16[256,3,128]{0,2,1:T(8,128)(2,1)S(1)} %pad_maximum_fusion.1), channel_id=1, source_target_pairs={{0,1},{1,2},{2,3},{3,0},{4,5},{5,6},{6,7},{7,4},{8,9},{9,10},{10,1... | collective-permute-start | bytes 589832 | tf_op jit(solution)/shard_map/ppermute | solution.py:17
  51.5 1.9 %copy-start.3 = (bf16[256,1,128]{2,0,1:T(8,128)(2,1)S(1)}, bf16[256,1,128]{2,0,1:T(8,128)(2,1)}, u32[]{:S(2)}) copy-start(bf16[256,1,128]{2,0,1:T(8,128)(2,1)} %param.23) | copy-start | bytes 196612
  52.6 0.8 copy-start.1
  57.4 116.7 %all-gather.3.cloned.1.call-start = ((), (), s32[]{:S(2)}) async-start(), calls=%async_computation.2 | async-start | bytes 2949120 | tf_op jit(solution)/shard_map/all_gather | solution.py:83
  139.0 2.1 %copy-start.4 = (bf16[256,1,128]{2,0,1:T(8,128)(2,1)S(1)}, bf16[256,1,128]{2,0,1:T(8,128)(2,1)}, u32[]{:S(2)}) copy-start(bf16[256,1,128]{2,0,1:T(8,128)(2,1)} %param.23) | copy-start | bytes 196612
  142.6 26.6 %copy-start.2 = (bf16[256,9,128]{2,0,1:T(8,128)(2,1)S(1)}, bf16[256,9,128]{2,0,1:T(8,128)(2,1)}, u32[]{:S(2)}) copy-start(bf16[256,9,128]{2,0,1:T(8,128)(2,1)} %copy-done.1) | copy-start | bytes 1769476
  142.6 11.9 %collective-permute-start.4 = (f32[256,3,128]{2,0,1:T(8,128)S(1)}, f32[256,3,128]{2,0,1:T(8,128)S(1)}, u32[]{:S(2)}, u32[]{:S(2)}) collective-permute-start(f32[256,3,128]{2,0,1:T(8,128)S(1)} %get-tuple-element.96), channel_id=1, source_target_pairs={{0,1},{1,2},{2,3},{3,0},{4,5},{5,6},{6,7},{7,4},{8,9},{9,10},{10,1... | collective-permute-start | bytes 1179656 | tf_op jit(solution)/shard_map/ppermute | solution.py:17
  143.9 19.4 %collective-permute-start.5 = (f32[256,3,128]{2,0,1:T(8,128)S(1)}, f32[256,3,128]{2,0,1:T(8,128)S(1)}, u32[]{:S(2)}, u32[]{:S(2)}) collective-permute-start(f32[256,3,128]{2,0,1:T(8,128)S(1)} %get-tuple-element.97), channel_id=1, source_target_pairs={{1,0},{2,1},{3,2},{0,3},{5,4},{6,5},{7,6},{4,7},{9,8},{10,9},{11,1... | collective-permute-start | bytes 1179656 | tf_op jit(solution)/shard_map/ppermute | solution.py:19
  163.4 7.0 %collective-permute-start.6 = (f32[256,1,128]{2,0,1:T(8,128)S(1)}, f32[256,1,128]{2,0,1:T(8,128)S(1)}, u32[]{:S(2)}, u32[]{:S(2)}) collective-permute-start(f32[256,1,128]{2,0,1:T(8,128)S(1)} %get-tuple-element.98), channel_id=1, source_target_pairs={{0,4},{4,8},{8,12},{1,5},{5,9},{9,13},{2,6},{6,10},{10,14},{3,7},{... | collective-permute-start | bytes 393224 | tf_op jit(solution)/shard_map/ppermute | solution.py:17
  167.2 6.3 %collective-permute-start.7 = (f32[256,1,128]{2,0,1:T(8,128)S(1)}, f32[256,1,128]{2,0,1:T(8,128)S(1)}, u32[]{:S(2)}, u32[]{:S(2)}) collective-permute-start(f32[256,1,128]{2,0,1:T(8,128)S(1)} %get-tuple-element.99), channel_id=1, source_target_pairs={{4,0},{8,4},{12,8},{5,1},{9,5},{13,9},{6,2},{10,6},{14,10},{7,3},{... | collective-permute-start | bytes 393224 | tf_op jit(solution)/shard_map/ppermute | solution.py:19
Sparse Core Ops, SparseCore 0:
  57.5 79.0 reduce-scatter.1
  139.1 24.9 all-gather.2
